TPU v7x, 512 devices: a whole 4x8x8 slice. The times are simulated.
512 devices in a mesh: seq: 64 (over z_hi, y, core), ch: 8 (over x, z_lo).
Axes of the slice: x: 4, y: 8, z: 8 (z_hi: 4, z_lo: 2; z = z_hi * 2 + z_lo), core: 2. Of those that a mesh axis runs over, the one named last changes fastest.
Arguments:
- inputs: bfloat16 [262144, 2048], P('seq', 'ch'), may hold values from -6 to 6
- first_factor: bfloat16 [512, 512], P('ch'), may hold values from -0.25 to 0.25
- twiddle: float32 [512, 512], P('seq'), may hold values from -4 to 4
- second_factor: bfloat16 [512, 512], P('ch'), may hold values from -0.25 to 0.25
- block_first: bfloat16 [64, 32, 32], P('ch'), may hold values from -1 to 1
- block_second: bfloat16 [32, 64, 64], P('ch'), may hold values from -0.75 to 0.75
Outputs:
- mixed_out: bfloat16 [262144, 2048], P('seq', 'ch')
All inputs are finite; a program needn't handle non-finite values.
Results may differ from a plain program's by a relative error of at most 0.007.
Values may be sent and summed in bfloat16 or wider, within the bound.
No kernel may reach another device: no remote copies, remote signals or barrier semaphores. Data moves between devices by JAX's collectives and lax.ppermute only.
A program may use at most 128 MiB of HBM per device.

v0:
```python
import jax
import jax.numpy as jnp
from jax import lax
from jax.sharding import PartitionSpec as P

BLOCK = 512


def local(inputs, first_factor, twiddle, second_factor, block_first, block_second):
    tok_rows, channels = inputs.shape
    outer_rows = tok_rows // BLOCK
    token_grid = inputs.reshape(outer_rows, BLOCK, channels)
    contract = (((1,), (1,)), ((), ()))
    first = lax.dot_general(
        lax.all_gather(first_factor, "ch", axis=0, tiled=True),
        token_grid,
        contract,
        preferred_element_type=jnp.float32,
    )
    full_second = lax.all_gather(second_factor, "ch", axis=0, tiled=True)
    twisted = (first * jnp.transpose(twiddle)[:, :, None]).astype(jnp.bfloat16)
    mixed = lax.dot_general(
        full_second,
        lax.all_to_all(twisted, "seq", split_axis=0, concat_axis=1, tiled=True),
        contract,
        preferred_element_type=jnp.float32,
    )
    second = mixed.astype(jnp.bfloat16)
    returned = lax.all_to_all(second, "seq", split_axis=0, concat_axis=1, tiled=True)
    gated = (token_grid.astype(jnp.float32) * returned.astype(jnp.float32)).astype(jnp.bfloat16)
    grouped = gated.reshape(tok_rows, block_first.shape[0], block_first.shape[2])
    block_mix = jnp.einsum(
        "amb,tab->mat", block_first, grouped, preferred_element_type=jnp.float32
    ).astype(jnp.bfloat16)
    result_rows = jnp.einsum(
        "mpa,mat->tmp",
        block_second,
        lax.all_to_all(block_mix, "ch", split_axis=0, concat_axis=1, tiled=True),
        preferred_element_type=jnp.float32,
    )
    return result_rows.reshape(tok_rows, channels).astype(jnp.bfloat16)


def solution(mesh):
    placed = (
        P("seq", "ch"),
        P("ch", None),
        P("seq", None),
        P("ch", None),
        P("ch", None, None),
        P("ch", None, None),
    )
    return jax.shard_map(
        local, mesh=mesh, in_specs=placed, out_specs=P("seq", "ch"), check_vma=False
    )
```

profile of v0, /device:TPU:41, one launch (start us, length us, event | category | flops | bytes accessed | tf_op | source)
XLA Modules:
  0.0 266.0 jit_solution(8618646083847221918)
XLA Ops:
  0.0 0.0 copy-start
  0.0 25.3 %all_gather.6 = bf16[512,512]{1,0:T(8,128)(2,1)S(1)} all-gather(bf16[64,512]{1,0:T(8,128)(2,1)} %param.7), channel_id=1, replica_groups=mesh['seq'=64,'ch'=8] {'ch'}, dimensions={0}, use_global_device_ids=true | all-gather | bytes 589824 | tf_op jit(solution)/shard_map/all_gather | solution.py:15
  25.3 3.1 %multiply_convert_fusion = bf16[512,8,256]{2,0,1:T(8,128)(2,1)S(1)} fusion(bf16[8,512,256]{2,1,0:T(8,128)(2,1)} %bitcast.44, f32[512,8]{0,1:T(8,128)} %bitcast.46, bf16[512,512]{1,0:T(8,128)(2,1)S(1)} %all_gather.6), kind=kOutput, calls=%fused_computation.6 | convolution fusion | flops 1075838976 | bytes 4734976 | tf_op jit(solution)/shard_map/dot_general | solution.py:14
  28.4 2.5 copy.30
  30.9 0.0 copy-start.3
  30.9 21.6 %all-to-all-start = ((bf16[512,8,256]{2,1,0:T(8,128)(2,1)}), bf16[512,8,256]{2,1,0:T(8,128)(2,1)S(1)}, u32[]{:S(2)}, u32[]{:S(2)}) async-start(bf16[512,8,256]{2,1,0:T(8,128)(2,1)} %copy.30), calls=%async_computation | async-start | bytes 4194304 | tf_op jit(solution)/shard_map/all_to_all | solution.py:24
  52.5 0.0 copy-done.3
  52.5 64.1 %all_gather.7 = bf16[512,512]{1,0:T(8,128)(2,1)S(1)} all-gather(bf16[64,512]{1,0:T(8,128)(2,1)S(1)} %copy-done.3), channel_id=1, replica_groups=mesh['seq'=64,'ch'=8] {'ch'}, dimensions={0}, use_global_device_ids=true | all-gather | bytes 589824 | tf_op jit(solution)/shard_map/all_gather | solution.py:20
  116.6 0.0 all-to-all-done
  116.6 2.6 convert_bitcast_fusion.1
  119.2 4.5 %copy.33 = bf16[512,8,256]{2,1,0:T(8,128)(2,1)} copy(bf16[512,8,256]{0,2,1:T(8,128)(2,1)} %convert_bitcast_fusion.1) | data formatting | bytes 4194304 | tf_op jit(solution)/shard_map/convert_element_type | solution.py:28
  123.7 22.9 %all-to-all-start.1 = ((bf16[512,8,256]{2,1,0:T(8,128)(2,1)}), bf16[512,8,256]{2,1,0:T(8,128)(2,1)S(1)}, u32[]{:S(2)}, u32[]{:S(2)}) async-start(bf16[512,8,256]{2,1,0:T(8,128)(2,1)} %copy.33), calls=%async_computation.1 | async-start | bytes 4194304 | tf_op jit(solution)/shard_map/all_to_all | solution.py:29
  146.6 4.1 %copy.29 = bf16[4096,256]{0,1:T(8,128)(2,1)} copy(bf16[4096,256]{1,0:T(8,128)(2,1)} %param.6) | data formatting | bytes 4194304 | tf_op args[0]
  150.7 50.4 %all-to-all-done.1 = bf16[512,8,256]{2,1,0:T(8,128)(2,1)S(1)} async-done(((bf16[512,8,256]{2,1,0:T(8,128)(2,1)}), bf16[512,8,256]{2,1,0:T(8,128)(2,1)S(1)}, u32[]{:S(2)}, u32[]{:S(2)}) %all-to-all-start.1) | async-done | bytes 2097184 | tf_op jit(solution)/shard_map/all_to_all | solution.py:29
  201.1 0.5 convert_bitcast_fusion
  201.6 2.3 copy.34
  204.0 10.9 %reshape.17 = f32[4096,8,32]{2,1,0:T(8,128)} reshape(f32[8,64,8,256]{3,2,1,0:T(8,128)} %copy.34) | data formatting | bytes 8388608 | tf_op jit(solution)/shard_map/convert_element_type | solution.py:30
  214.9 0.0 copy-start.1
  214.9 11.6 %copy.35 = f32[4096,8,32]{0,2,1:T(8,128)} copy(f32[4096,8,32]{2,1,0:T(8,128)} %reshape.17) | data formatting | bytes 8388608 | tf_op jit(solution)/shard_map/convert_element_type | solution.py:30
  226.4 0.0 copy-done
  226.4 0.0 copy-done.1
  226.4 2.9 %fusion = bf16[32,8,4096]{2,0,1:T(8,128)(2,1)S(1)} fusion(bf16[8,32,32]{2,1,0:T(8,128)(2,1)S(1)} %copy-done, f32[4096,8,32]{0,2,1:T(8,128)} %copy.35, bf16[4096,8,32]{0,2,1:T(8,128)(2,1)S(1)} %bitcast.43), kind=kOutput, calls=%fused_computation.2 | convolution fusion | flops 71303168 | bytes 8404992 | tf_op jit(solution)/shard_map/amb,tab->mat/dot_general | solution.py:32
  229.3 1.2 copy.36
  230.5 0.0 copy-start.2
  230.5 32.3 %all_to_all.45 = bf16[32,8,4096]{2,1,0:T(8,128)(2,1)S(1)} all-to-all(bf16[32,8,4096]{2,1,0:T(8,128)(2,1)S(1)} %copy.36), channel_id=1, replica_groups=mesh['seq'=64,'ch'=8] {'ch'}, dimensions={0} | all-to-all | bytes 4194304 | tf_op jit(solution)/shard_map/all_to_all | solution.py:38
  262.8 0.0 copy-done.2
  262.8 0.7 convolution_convert_fusion
  263.5 2.5 copy.38
Async XLA Ops:
  0.0 226.4 %copy-start = (bf16[8,32,32]{2,1,0:T(8,128)(2,1)S(1)}, bf16[8,32,32]{2,1,0:T(8,128)(2,1)}, u32[]{:S(2)}) copy-start(bf16[8,32,32]{2,1,0:T(8,128)(2,1)} %param.10) | copy-start | bytes 49156
  30.9 21.6 %copy-start.3 = (bf16[64,512]{1,0:T(8,128)(2,1)S(1)}, bf16[64,512]{1,0:T(8,128)(2,1)}, u32[]{:S(2)}) copy-start(bf16[64,512]{1,0:T(8,128)(2,1)} %param.9) | copy-start | bytes 196612
  30.9 85.7 %all-to-all-start = ((bf16[512,8,256]{2,1,0:T(8,128)(2,1)}), bf16[512,8,256]{2,1,0:T(8,128)(2,1)S(1)}, u32[]{:S(2)}, u32[]{:S(2)}) async-start(bf16[512,8,256]{2,1,0:T(8,128)(2,1)} %copy.30), calls=%async_computation | async-start | bytes 4194304 | tf_op jit(solution)/shard_map/all_to_all | solution.py:24
  123.7 77.4 %all-to-all-start.1 = ((bf16[512,8,256]{2,1,0:T(8,128)(2,1)}), bf16[512,8,256]{2,1,0:T(8,128)(2,1)S(1)}, u32[]{:S(2)}, u32[]{:S(2)}) async-start(bf16[512,8,256]{2,1,0:T(8,128)(2,1)} %copy.33), calls=%async_computation.1 | async-start | bytes 4194304 | tf_op jit(solution)/shard_map/all_to_all | solution.py:29
  214.9 11.6 %copy-start.1 = (bf16[4096,256]{0,1:T(8,128)(2,1)S(1)}, bf16[4096,256]{0,1:T(8,128)(2,1)}, u32[]{:S(2)}) copy-start(bf16[4096,256]{0,1:T(8,128)(2,1)} %copy.29) | copy-start | bytes 6291460
  230.5 32.4 %copy-start.2 = (bf16[4,64,64]{2,1,0:T(8,128)(2,1)S(1)}, bf16[4,64,64]{2,1,0:T(8,128)(2,1)}, u32[]{:S(2)}) copy-start(bf16[4,64,64]{2,1,0:T(8,128)(2,1)} %param.11) | copy-start | bytes 98308
where the time goes:
time: 267 us; the launch traced here: 266 us
  blocking collectives  122 us (46%)
  waiting for transfers between devices  50.4 us (19%)
  starting transfers between devices  44.5 us (17%)
  local copies, waits for them, and re-layouts  39.5 us (15%)
  matrix products  9.27 us (3%)
    all_gather x1, blocking collectives, local(): full_second = lax.all_gather(second_factor, 'ch', axis=0, tiled=True)  64.1 us
    all_to_all x1, waiting for transfers between devices, local(): lax.all_to_all(second, 'seq', split_axis=0, concat_axis=1, tiled=True)  50.4 us
    all_to_all x1, blocking collectives, local(): lax.all_to_all(block_mix, 'ch', split_axis=0, concat_axis=1, tiled=True)  32.3 us
    all_gather x1, blocking collectives, local(): lax.all_gather(first_factor, 'ch', axis=0, tiled=True)  25.3 us
    convert_element_type x3, local copies, waits for them, and re-layouts, local(): returned.astype(jnp.float32)  24.8 us
    all_to_all x1, starting transfers between devices, local(): lax.all_to_all(second, 'seq', split_axis=0, concat_axis=1, tiled=True)  22.9 us
    all_to_all x1, starting transfers between devices, local(): lax.all_to_all(twisted, 'seq', split_axis=0, concat_axis=1, tiled=True)  21.6 us
  transfers between devices with their start and end apart: 2, of which 1 were waited for; matrix products, arithmetic and copies ran while one was open for 2% of the time, Pallas kernels for 0%

commit v1 on v0

--- a/solution.py
+++ b/solution.py
@@ -17,7 +17,8 @@
         contract,
         preferred_element_type=jnp.float32,
     )
-    full_second = lax.all_gather(second_factor, "ch", axis=0, tiled=True)
+    outgoing = jnp.stack([second_factor] * lax.axis_size("ch"))
+    full_second = jnp.concatenate(lax.all_to_all(outgoing, "ch", 0, 0), axis=0)
     twisted = (first * jnp.transpose(twiddle)[:, :, None]).astype(jnp.bfloat16)
     mixed = lax.dot_general(
         full_second,

time: 267 us -> 250 us (0.936)
  starting transfers between devices: 44.5 us -> 15.3 us
  blocking collectives: 122 us -> 138 us
  matrix products: 9.27 us -> 6.36 us
    all_to_all x0 -> x1, blocking collectives: none -> 74.4 us  [local(): lax.all_to_all(twisted, 'seq', split_axis=0, concat_axis=1, tiled=True)]
    all_gather x1 -> x0, blocking collectives: 64.1 us -> none  [local(): full_second = lax.all_gather(second_factor, 'ch', axis=0, tiled=True)]
    all_to_all x1, starting transfers between devices: 21.6 us -> 5.83 us  [local(): full_second = jnp.concatenate(lax.all_to_all(outgoing, 'ch', 0, 0), axis=0)]
    all_to_all x1, starting transfers between devices: 22.9 us -> 9.49 us  [local(): lax.all_to_all(second, 'seq', split_axis=0, concat_axis=1, tiled=True)]
    all_to_all x1, blocking collectives: 32.3 us -> 35.8 us  [local(): lax.all_to_all(block_mix, 'ch', split_axis=0, concat_axis=1, tiled=True)]
    all_gather x1, blocking collectives: 25.3 us -> 28.2 us  [local(): lax.all_gather(first_factor, 'ch', axis=0, tiled=True)]
  transfers between devices with their start and end apart: 2 -> 2, of which waited for: 1 -> 1; matrix products, arithmetic and copies ran while one was open for 2% -> 3% of each run, Pallas kernels for 0% -> 0%
where the time goes in v1:
time: 250 us; the launch traced here: 249 us
  blocking collectives  138 us (55%)
  waiting for transfers between devices  49.5 us (20%)
  local copies, waits for them, and re-layouts  38.6 us (15%)
  starting transfers between devices  15.3 us (6%)
  matrix products  6.36 us (3%)
    all_to_all x1, blocking collectives, local(): lax.all_to_all(twisted, 'seq', split_axis=0, concat_axis=1, tiled=True)  74.4 us
    all_to_all x1, waiting for transfers between devices, local(): lax.all_to_all(second, 'seq', split_axis=0, concat_axis=1, tiled=True)  49.5 us
    all_to_all x1, blocking collectives, local(): lax.all_to_all(block_mix, 'ch', split_axis=0, concat_axis=1, tiled=True)  35.8 us
    all_gather x1, blocking collectives, local(): lax.all_gather(first_factor, 'ch', axis=0, tiled=True)  28.2 us
    convert_element_type x3, local copies, waits for them, and re-layouts, local(): returned.astype(jnp.float32)  24.8 us
    all_to_all x1, starting transfers between devices, local(): lax.all_to_all(second, 'seq', split_axis=0, concat_axis=1, tiled=True)  9.49 us
    all_to_all x1, starting transfers between devices, local(): full_second = jnp.concatenate(lax.all_to_all(outgoing, 'ch', 0, 0), axis=0)  5.83 us
  transfers between devices with their start and end apart: 2, of which 1 were waited for; matrix products, arithmetic and copies ran while one was open for 3% of the time, Pallas kernels for 0%

profile of v1, /device:TPU:41, one launch (start us, length us, event | category | flops | bytes accessed | tf_op | source)
XLA Modules:
  0.0 248.7 jit_solution(16546563243238842508)
XLA Ops:
  0.0 0.0 copy-start
  0.0 0.0 copy-start.2
  0.0 0.0 copy-start.4
  0.0 1.8 stack.2
  1.8 5.8 %all-to-all-start.1 = ((bf16[8,64,512]{2,1,0:T(8,128)(2,1)}), bf16[8,64,512]{2,1,0:T(8,128)(2,1)S(1)}, u32[]{:S(2)}, u32[]{:S(2)}) async-start(bf16[8,64,512]{2,1,0:T(8,128)(2,1)} %stack.2), calls=%async_computation.1 | async-start | bytes 1048576 | tf_op jit(solution)/shard_map/all_to_all | solution.py:21
  7.7 28.2 %all_gather.3 = bf16[512,512]{1,0:T(8,128)(2,1)S(1)} all-gather(bf16[64,512]{1,0:T(8,128)(2,1)} %param.7), channel_id=1, replica_groups=mesh['seq'=64,'ch'=8] {'ch'}, dimensions={0}, use_global_device_ids=true | all-gather | bytes 589824 | tf_op jit(solution)/shard_map/all_gather | solution.py:15
  35.9 0.0 copy-done.2
  35.9 0.0 copy-done.4
  35.9 1.5 multiply_convert_fusion
  37.3 1.2 copy.30
  38.5 0.0 all-to-all-done.1
  38.5 74.4 %all_to_all.50 = bf16[512,8,256]{2,1,0:T(8,128)(2,1)S(1)} all-to-all(bf16[512,8,256]{2,1,0:T(8,128)(2,1)S(1)} %copy.30), channel_id=1, replica_groups=mesh['seq'=64,'ch'=8] {'seq'}, dimensions={0} | all-to-all | bytes 4194304 | tf_op jit(solution)/shard_map/all_to_all | solution.py:25
  112.9 1.3 convert_bitcast_fusion.1
  114.3 3.1 %copy.33 = bf16[512,8,256]{2,1,0:T(8,128)(2,1)} copy(bf16[512,8,256]{0,2,1:T(8,128)(2,1)S(1)} %convert_bitcast_fusion.1) | data formatting | bytes 4194304 | tf_op jit(solution)/shard_map/convert_element_type | solution.py:29
  117.3 9.5 %all-to-all-start.2 = ((bf16[512,8,256]{2,1,0:T(8,128)(2,1)}), bf16[512,8,256]{2,1,0:T(8,128)(2,1)S(1)}, u32[]{:S(2)}, u32[]{:S(2)}) async-start(bf16[512,8,256]{2,1,0:T(8,128)(2,1)} %copy.33), calls=%async_computation.2 | async-start | bytes 4194304 | tf_op jit(solution)/shard_map/all_to_all | solution.py:30
  126.8 4.1 %copy.29 = bf16[4096,256]{0,1:T(8,128)(2,1)} copy(bf16[4096,256]{1,0:T(8,128)(2,1)} %param.6) | data formatting | bytes 4194304 | tf_op args[0]
  130.9 49.5 %all-to-all-done.2 = bf16[512,8,256]{2,1,0:T(8,128)(2,1)S(1)} async-done(((bf16[512,8,256]{2,1,0:T(8,128)(2,1)}), bf16[512,8,256]{2,1,0:T(8,128)(2,1)S(1)}, u32[]{:S(2)}, u32[]{:S(2)}) %all-to-all-start.2) | async-done | bytes 2097184 | tf_op jit(solution)/shard_map/all_to_all | solution.py:30
  180.4 0.5 convert_bitcast_fusion
  180.9 2.3 copy.34
  183.3 10.9 %reshape.23 = f32[4096,8,32]{2,1,0:T(8,128)} reshape(f32[8,64,8,256]{3,2,1,0:T(8,128)} %copy.34) | data formatting | bytes 8388608 | tf_op jit(solution)/shard_map/convert_element_type | solution.py:31
  194.2 0.0 copy-start.1
  194.2 11.6 %copy.35 = f32[4096,8,32]{0,2,1:T(8,128)} copy(f32[4096,8,32]{2,1,0:T(8,128)} %reshape.23) | data formatting | bytes 8388608 | tf_op jit(solution)/shard_map/convert_element_type | solution.py:31
  205.8 0.0 copy-done
  205.8 0.0 copy-done.1
  205.8 2.9 %fusion = bf16[32,8,4096]{2,0,1:T(8,128)(2,1)S(1)} fusion(bf16[8,32,32]{2,1,0:T(8,128)(2,1)S(1)} %copy-done, f32[4096,8,32]{0,2,1:T(8,128)} %copy.35, bf16[4096,8,32]{0,2,1:T(8,128)(2,1)S(1)} %bitcast.44), kind=kOutput, calls=%fused_computation.2 | convolution fusion | flops 71303168 | bytes 8404992 | tf_op jit(solution)/shard_map/amb,tab->mat/dot_general | solution.py:33
  208.7 1.2 copy.36
  209.8 0.0 copy-start.3
  209.8 35.8 %all_to_all.51 = bf16[32,8,4096]{2,1,0:T(8,128)(2,1)S(1)} all-to-all(bf16[32,8,4096]{2,1,0:T(8,128)(2,1)S(1)} %copy.36), channel_id=1, replica_groups=mesh['seq'=64,'ch'=8] {'ch'}, dimensions={0} | all-to-all | bytes 4194304 | tf_op jit(solution)/shard_map/all_to_all | solution.py:39
  245.6 0.0 copy-done.3
  245.6 0.7 convolution_convert_fusion
  246.3 2.5 copy.38
Async XLA Ops:
  0.0 205.8 %copy-start = (bf16[8,32,32]{2,1,0:T(8,128)(2,1)S(1)}, bf16[8,32,32]{2,1,0:T(8,128)(2,1)}, u32[]{:S(2)}) copy-start(bf16[8,32,32]{2,1,0:T(8,128)(2,1)} %param.10) | copy-start | bytes 49156
  0.0 35.9 %copy-start.2 = (bf16[4096,256]{1,0:T(8,128)(2,1)S(1)}, bf16[4096,256]{1,0:T(8,128)(2,1)}, u32[]{:S(2)}) copy-start(bf16[4096,256]{1,0:T(8,128)(2,1)} %param.6) | copy-start | bytes 6291460
  0.0 35.9 %copy-start.4 = (f32[8,512]{1,0:T(8,128)S(1)}, f32[8,512]{1,0:T(8,128)}, u32[]{:S(2)}) copy-start(f32[8,512]{1,0:T(8,128)} %param.8) | copy-start | bytes 49156
  1.8 36.7 %all-to-all-start.1 = ((bf16[8,64,512]{2,1,0:T(8,128)(2,1)}), bf16[8,64,512]{2,1,0:T(8,128)(2,1)S(1)}, u32[]{:S(2)}, u32[]{:S(2)}) async-start(bf16[8,64,512]{2,1,0:T(8,128)(2,1)} %stack.2), calls=%async_computation.1 | async-start | bytes 1048576 | tf_op jit(solution)/shard_map/all_to_all | solution.py:21
  117.3 63.0 %all-to-all-start.2 = ((bf16[512,8,256]{2,1,0:T(8,128)(2,1)}), bf16[512,8,256]{2,1,0:T(8,128)(2,1)S(1)}, u32[]{:S(2)}, u32[]{:S(2)}) async-start(bf16[512,8,256]{2,1,0:T(8,128)(2,1)} %copy.33), calls=%async_computation.2 | async-start | bytes 4194304 | tf_op jit(solution)/shard_map/all_to_all | solution.py:30
  194.2 11.6 %copy-start.1 = (bf16[4096,256]{0,1:T(8,128)(2,1)S(1)}, bf16[4096,256]{0,1:T(8,128)(2,1)}, u32[]{:S(2)}) copy-start(bf16[4096,256]{0,1:T(8,128)(2,1)} %copy.29) | copy-start | bytes 6291460
  209.8 35.8 %copy-start.3 = (bf16[4,64,64]{2,1,0:T(8,128)(2,1)S(1)}, bf16[4,64,64]{2,1,0:T(8,128)(2,1)}, u32[]{:S(2)}) copy-start(bf16[4,64,64]{2,1,0:T(8,128)(2,1)} %param.11) | copy-start | bytes 98308
